TPU v7x, 32 devices: a whole 2x2x4 slice. The times are simulated.
32 devices in a mesh: row: 8 (over z, y), rep: 4 (over x, core).
Axes of the slice: x: 2, y: 2, z: 4, core: 2. Of those that a mesh axis runs over, the one named last changes fastest.
Arguments:
- features: bfloat16 [2048, 256], P('row'), may hold values from -6 to 6
- cotangent: bfloat16 [2048, 256], P('row'), may hold values from -0.3125 to 0.3125
- weight_one: bfloat16 [256, 256], replicated, may hold values from -0.375 to 0.375
- weight_two: bfloat16 [256, 256], replicated, may hold values from -0.375 to 0.375
- block_index: int32 [8, 4, 2, 4], P('row', 'rep'), may hold values from 0 to 15, as said below
- block_count: int32 [8, 4, 2], P('row', 'rep'), may hold values from 0 to 4
- block_values: bfloat16 [8, 4, 2, 4, 128, 128], P('row', 'rep'), as said below
Outputs:
- logits: bfloat16 [2048, 256], P(('row', 'rep'))
- grad_one: float32 [256, 256], replicated
- grad_two: float32 [256, 256], replicated
Inputs may be any that keep to these rules, and one draw needn't show every extreme that they name: block_index[i, j, a, s] lies in [j * 4, (j + 1) * 4); for s < block_count[i, j, a] the entries rise strictly; later entries equal j * 4 and are not part of A. `block_values`: A is symmetric: block (r, c) is listed exactly when block (c, r) is, and its entries are the transpose of those of block (c, r). Entries are normal with standard deviation (0.5 * 128 * 16) ** -0.5, cut at five such deviations; blocks on the diagonal are symmetric.
All inputs are finite; a program needn't handle non-finite values.
Results may differ from a plain program's by a relative error of at most 0.0059.
Values may be sent and summed in bfloat16 or wider, within the bound.
No kernel may reach another device: no remote copies, remote signals or barrier semaphores. Data moves between devices by JAX's collectives and lax.ppermute only.
A program may use at most 64 MiB of HBM per device.

v0:
```python
import jax
import jax.numpy as jnp
from jax import lax
from jax.sharding import PartitionSpec as P


def broadcast(array, axis, root):
    mine = lax.axis_index(axis) == root
    return lax.psum(jnp.where(mine, array, jnp.zeros_like(array)), axis)


def aggregate(source, block_index, block_count, block_values):
    copies = lax.axis_size("rep")
    sections = lax.axis_size("row") // copies
    copy_index = lax.axis_index("rep")
    node_rows, feature_width = source.shape
    block_rows = block_values.shape[2]
    slot_count = block_values.shape[3]
    block_side = block_values.shape[-1]

    def fetch(state_unused, section_index):
        panel = broadcast(source, "row", copy_index * sections + section_index)
        return (state_unused, panel)

    state_unused, panels = lax.scan(fetch, jnp.int32(0), jnp.arange(sections, dtype=jnp.int32))
    panels = panels.reshape(sections * block_rows, block_side, feature_width)
    columns = block_index[0, 0] - copy_index * slot_count
    live_slots = jnp.arange(slot_count, dtype=jnp.int32)[None, :] < block_count[0, 0][:, None]
    picked = jnp.take(panels, columns.reshape(-1), axis=0).reshape(
        block_rows, slot_count, block_side, feature_width
    )
    picked = jnp.where(live_slots[:, :, None, None], picked, jnp.zeros((), picked.dtype))
    partial_value = lax.dot_general(
        block_values[0, 0],
        picked,
        (((1, 3), (1, 2)), ((0,), (0,))),
        preferred_element_type=jnp.float32,
    )
    partial_value = partial_value.reshape(node_rows, feature_width)
    result = lax.psum(partial_value, "rep")
    return result


def shards(features, cotangent, weight_one, weight_two, block_index, block_count, block_values):
    copies = lax.axis_size("rep")
    copy_index = lax.axis_index("rep")
    node_rows = features.shape[0]
    share_rows = node_rows // copies
    first_row = copy_index * share_rows

    def own_rows(array):
        return lax.dynamic_slice_in_dim(array, first_row, share_rows, 0)

    agg_one = aggregate(features, block_index, block_count, block_values).astype(jnp.bfloat16)
    pre_one = jnp.dot(agg_one, weight_one, preferred_element_type=jnp.float32)
    hidden = jax.nn.silu(pre_one).astype(jnp.bfloat16)
    agg_two = aggregate(hidden, block_index, block_count, block_values).astype(jnp.bfloat16)
    agg_two_own = own_rows(agg_two)
    logits = jnp.dot(agg_two_own, weight_two, preferred_element_type=jnp.float32).astype(
        jnp.bfloat16
    )
    cotangent_own = own_rows(cotangent)
    grad_two = lax.dot_general(
        agg_two_own, cotangent_own, (((0,), (0,)), ((), ())), preferred_element_type=jnp.float32
    )
    grad_two = lax.psum(grad_two, ("row", "rep"))
    back_signal = lax.dot_general(
        cotangent, weight_two, (((1,), (1,)), ((), ())), preferred_element_type=jnp.float32
    ).astype(jnp.bfloat16)
    carried = aggregate(back_signal, block_index, block_count, block_values)
    carried = own_rows(carried)
    pre_own = own_rows(pre_one)
    agg_one_own = own_rows(agg_one)
    gate_value = jax.nn.sigmoid(pre_own)
    pre_grad = (carried * (gate_value + pre_own * gate_value * (1.0 - gate_value))).astype(
        jnp.bfloat16
    )
    grad_one = lax.dot_general(
        agg_one_own, pre_grad, (((0,), (0,)), ((), ())), preferred_element_type=jnp.float32
    )
    grad_one = lax.psum(grad_one, ("row", "rep"))
    return (logits, grad_one, grad_two)


def solution(mesh):
    in_specs = (
        P("row", None),
        P("row", None),
        P(),
        P(),
        P("row", "rep", None, None),
        P("row", "rep", None),
        P("row", "rep", None, None, None, None),
    )
    out_specs = (P(("row", "rep"), None), P(), P())
    return jax.shard_map(shards, mesh=mesh, in_specs=in_specs, out_specs=out_specs, check_vma=False)
```

profile of v0, /device:TPU:0, one launch (start us, length us, event | category | flops | bytes accessed | tf_op | source)
XLA Modules:
  0.0 661.8 jit_solution(11847135036822304722)
XLA Ops:
  8.0 0.7 copy-done.4
  8.9 1.2 convolution_convert_fusion
  10.1 154.0 %while.38 = (s32[]{:T(128)}, bf16[2,256,256]{2,1,0:T(8,128)(2,1)S(1)}, s32[2]{0:T(128)S(1)}, s32[]{:T(128)}, bf16[256,256]{1,0:T(8,128)(2,1)S(1)}, /*index=5*/s32[]{:T(128)}, u32[]{:T(128)}, u32[]{:T(128)}) while((s32[]{:T(128)}, bf16[2,256,256]{2,1,0:T(8,128)(2,1)S(1)}, s32[2]{0:T(128)S(1)}, s32[]{:T(128)}, ...), condition=%wide.region_10.12_spmd, body=%wide.region_8.11_spmd.sunk | while | flops 131079 | bytes 1310923 | solution.py:25
  10.2 0.6 dynamic_slice.53
  11.4 0.7 select_bitcast_fusion.8
  12.1 75.9 %all-reduce.17.cloned.1.call-done = bf16[1,256,256]{2,1,0:T(8,128)(2,1)} async-done(((bf16[1,256,256]{2,1,0:T(8,128)(2,1)}), bf16[1,256,256]{2,1,0:T(8,128)(2,1)}) %all-reduce.17.cloned.1.call-update) | async-done | bytes 131088 | tf_op jit(solution)/shard_map/while/body/eval_jaxpr/psum | solution.py:9
  88.0 0.9 constant_dynamic-update-slice_fusion.8
  89.0 0.6 dynamic_slice.53
  90.2 0.7 select_bitcast_fusion.8
  90.9 72.3 %all-reduce.17.cloned.1.call-done = bf16[1,256,256]{2,1,0:T(8,128)(2,1)} async-done(((bf16[1,256,256]{2,1,0:T(8,128)(2,1)}), bf16[1,256,256]{2,1,0:T(8,128)(2,1)}) %all-reduce.17.cloned.1.call-update) | async-done | bytes 131088 | tf_op jit(solution)/shard_map/while/body/eval_jaxpr/psum | solution.py:9
  163.2 0.9 constant_dynamic-update-slice_fusion.8
  164.1 0.6 gather_fusion.2
  164.7 0.9 copy-done.1
  165.6 150.0 %while.36 = (s32[]{:T(128)}, bf16[2,256,256]{2,1,0:T(8,128)(2,1)S(1)}, s32[2]{0:T(128)S(1)}, s32[]{:T(128)}, bf16[256,256]{1,0:T(8,128)(2,1)S(1)}, /*index=5*/s32[]{:T(128)}, u32[]{:T(128)}, u32[]{:T(128)}) while((s32[]{:T(128)}, bf16[2,256,256]{2,1,0:T(8,128)(2,1)S(1)}, s32[2]{0:T(128)S(1)}, s32[]{:T(128)}, bf16[256,256]{1,0:T(8,128)(2,1)S(1)}, ...), condition=%wide.region_2.3_spmd, body=%wide.region_0.2_spmd.sunk | while | flops 131079 | bytes 1310923 | solution.py:25
  165.6 0.6 dynamic_slice.51
  166.8 0.7 select_bitcast_fusion.6
  167.5 72.3 %all-reduce.13.cloned.1.call-done = bf16[1,256,256]{2,1,0:T(8,128)(2,1)} async-done(((bf16[1,256,256]{2,1,0:T(8,128)(2,1)}), bf16[1,256,256]{2,1,0:T(8,128)(2,1)}) %all-reduce.13.cloned.1.call-update) | async-done | bytes 131088 | tf_op jit(solution)/shard_map/while/body/eval_jaxpr/psum | solution.py:9
  239.8 0.9 constant_dynamic-update-slice_fusion.6
  240.8 0.6 dynamic_slice.51
  242.1 0.7 select_bitcast_fusion.6
  242.8 71.9 %all-reduce.13.cloned.1.call-done = bf16[1,256,256]{2,1,0:T(8,128)(2,1)} async-done(((bf16[1,256,256]{2,1,0:T(8,128)(2,1)}), bf16[1,256,256]{2,1,0:T(8,128)(2,1)}) %all-reduce.13.cloned.1.call-update) | async-done | bytes 131088 | tf_op jit(solution)/shard_map/while/body/eval_jaxpr/psum | solution.py:9
  314.7 0.9 constant_dynamic-update-slice_fusion.6
  315.6 0.6 gather_fusion
  316.2 0.6 copy-done.6
  317.1 0.3 fusion.4
  317.4 13.1 %all-reduce.18 = bf16[256,256]{1,0:T(8,128)(2,1)S(1)} all-reduce(f32[256,256]{1,0:T(8,128)S(1)} %bitcast.65), channel_id=1, replica_groups=mesh['row'=8,'rep'=4] {'rep'}, use_global_device_ids=true, to_apply=%region_3.5 | all-reduce | flops 65536 | bytes 393216 | tf_op jit(solution)/shard_map/psum | solution.py:40
  330.5 1.0 fusion
  331.8 150.5 %while.37 = (s32[]{:T(128)}, bf16[2,256,256]{2,1,0:T(8,128)(2,1)S(1)}, s32[2]{0:T(128)S(1)}, s32[]{:T(128)}, bf16[256,256]{1,0:T(8,128)(2,1)S(1)}, /*index=5*/s32[]{:T(128)}, u32[]{:T(128)}, u32[]{:T(128)}) while((s32[]{:T(128)}, bf16[2,256,256]{2,1,0:T(8,128)(2,1)S(1)}, s32[2]{0:T(128)S(1)}, s32[]{:T(128)}, bf16[256,256]{1,0:T(8,128)(2,1)S(1)}, ...), condition=%wide.region_6.8_spmd, body=%wide.region_4.7_spmd.sunk | while | flops 131079 | bytes 1310923 | solution.py:25
  331.9 0.6 dynamic_slice.52
  333.1 0.7 select_bitcast_fusion.7
  333.8 72.7 %all-reduce.15.cloned.1.call-done = bf16[1,256,256]{2,1,0:T(8,128)(2,1)} async-done(((bf16[1,256,256]{2,1,0:T(8,128)(2,1)}), bf16[1,256,256]{2,1,0:T(8,128)(2,1)}) %all-reduce.15.cloned.1.call-update) | async-done | bytes 131088 | tf_op jit(solution)/shard_map/while/body/eval_jaxpr/psum | solution.py:9
  406.5 0.9 constant_dynamic-update-slice_fusion.7
  407.5 0.6 dynamic_slice.52
  408.8 0.7 select_bitcast_fusion.7
  409.5 71.9 %all-reduce.15.cloned.1.call-done = bf16[1,256,256]{2,1,0:T(8,128)(2,1)} async-done(((bf16[1,256,256]{2,1,0:T(8,128)(2,1)}), bf16[1,256,256]{2,1,0:T(8,128)(2,1)}) %all-reduce.15.cloned.1.call-update) | async-done | bytes 131088 | tf_op jit(solution)/shard_map/while/body/eval_jaxpr/psum | solution.py:9
  481.4 0.9 constant_dynamic-update-slice_fusion.7
  482.4 0.5 all-reduce.9.cloned.1.call-update
  483.0 0.6 gather_fusion.1
  483.7 0.3 fusion.2
  484.0 13.8 %all-reduce.19 = bf16[256,256]{1,0:T(8,128)(2,1)S(1)} all-reduce(f32[256,256]{1,0:T(8,128)S(1)} %bitcast.64), channel_id=1, replica_groups=mesh['row'=8,'rep'=4] {'rep'}, use_global_device_ids=true, to_apply=%region_7.9 | all-reduce | flops 65536 | bytes 393216 | tf_op jit(solution)/shard_map/psum | solution.py:40
  497.7 1.7 fusion.16
  499.4 17.9 %all-reduce.9.cloned.1.call-done = f32[256,256]{1,0:T(8,128)} async-done(((f32[256,256]{1,0:T(8,128)}), f32[256,256]{1,0:T(8,128)}) %all-reduce.9.cloned.1.call-update) | async-done | bytes 262160 | tf_op jit(solution)/shard_map/psum | solution.py:40
  517.3 1.8 fusion.15
  519.1 0.9 copy-done.2
  519.9 0.8 convolution_convert_fusion.1
  520.7 131.2 %all-reduce.11.cloned.1.call-done = (f32[256,256]{1,0:T(8,128)}, f32[256,256]{1,0:T(8,128)}) async-done(((f32[256,256]{1,0:T(8,128)}, f32[256,256]{1,0:T(8,128)}), (f32[256,256]{1,0:T(8,128)}, f32[256,256]{1,0:T(8,128)})) %all-reduce.11.cloned.1.call-update) | async-done | bytes 524304 | tf_op jit(solution)/shard_map/psum | solution.py:81
  651.9 1.7 copy.44
  653.6 0.7 copy.45
  (40 shorter events, 1.2 us)
Async XLA Ops:
  8.0 309.1 %copy-start = (bf16[1,1,2,4,128,128]{5,4,3,2,1,0:T(8,128)(2,1)S(1)}, bf16[1,1,2,4,128,128]{5,4,3,2,1,0:T(8,128)(2,1)}, u32[]{:S(2)}) copy-start(bf16[1,1,2,4,128,128]{5,4,3,2,1,0:T(8,128)(2,1)} %param.21) | copy-start | bytes 786436
  8.0 0.7 copy-start.4
  10.1 77.9 %all-reduce.17.cloned.1.call-start = ((), (), s32[]{:S(2)}) async-start(), calls=%async_computation.4 | async-start | bytes 262144 | tf_op jit(solution)/shard_map/while/body/eval_jaxpr/psum | solution.py:9
  88.9 74.3 %all-reduce.17.cloned.1.call-start = ((), (), s32[]{:S(2)}) async-start(), calls=%async_computation.4 | async-start | bytes 262144 | tf_op jit(solution)/shard_map/while/body/eval_jaxpr/psum | solution.py:9
  164.7 0.9 copy-start.1
  165.6 74.2 %all-reduce.13.cloned.1.call-start = ((), (), s32[]{:S(2)}) async-start(), calls=%async_computation.2 | async-start | bytes 262144 | tf_op jit(solution)/shard_map/while/body/eval_jaxpr/psum | solution.py:9
  240.8 73.9 %all-reduce.13.cloned.1.call-start = ((), (), s32[]{:S(2)}) async-start(), calls=%async_computation.2 | async-start | bytes 262144 | tf_op jit(solution)/shard_map/while/body/eval_jaxpr/psum | solution.py:9
  316.2 0.7 copy-start.6
  330.5 1.0 copy-start.5
  331.8 74.7 %all-reduce.15.cloned.1.call-start = ((), (), s32[]{:S(2)}) async-start(), calls=%async_computation.3 | async-start | bytes 262144 | tf_op jit(solution)/shard_map/while/body/eval_jaxpr/psum | solution.py:9
  407.5 73.9 %all-reduce.15.cloned.1.call-start = ((), (), s32[]{:S(2)}) async-start(), calls=%async_computation.3 | async-start | bytes 262144 | tf_op jit(solution)/shard_map/while/body/eval_jaxpr/psum | solution.py:9
  482.3 35.0 %all-reduce.9.cloned.1.call-start = ((), (), s32[]{:S(2)}) async-start(), calls=%async_computation | async-start | bytes 524288 | tf_op jit(solution)/shard_map/psum | solution.py:40
  482.9 169.0 %all-reduce.11.cloned.1.call-start = ((), (), s32[]{:S(2)}) async-start(), calls=%async_computation.1 | async-start | bytes 1048576 | tf_op jit(solution)/shard_map/psum | solution.py:81
  519.0 0.9 copy-start.2
  651.9 1.7 copy-start.3
Sparse Core Ops, SparseCore 0:
  14.8 73.1 all-reduce.16
  93.6 69.4 all-reduce.16
  170.3 69.4 all-reduce.12
  245.2 69.4 all-reduce.12
  336.2 70.2 all-reduce.14
  411.9 69.4 all-reduce.14
Sparse Core Ops, SparseCore 1:
  485.7 31.5 all-reduce.8
  523.2 128.7 all-reduce.10
where the time goes:
time: 662 us
  waiting for transfers between devices  587 us (89%)
  blocking collectives  26.8 us (4%)
  local copies, waits for them, and re-layouts  16.4 us (2%)
  between operations  15.7 us (2%)
  matrix products  7.22 us (1%)
    psum x6, waiting for transfers between devices, broadcast(): return lax.psum(jnp.where(mine, array, jnp.zeros_like(array)), axis)  437 us
    psum x1, waiting for transfers between devices, shards(): grad_one = lax.psum(grad_one, ('row', 'rep'))  131 us
    psum x2, blocking collectives, aggregate(): result = lax.psum(partial_value, 'rep')  26.8 us
    psum x1, waiting for transfers between devices, aggregate(): result = lax.psum(partial_value, 'rep')  17.9 us
  transfers between devices with their start and end apart: 8, of which 8 were waited for; matrix products, arithmetic and copies ran while one was open for 1% of the time, Pallas kernels for 0%

commit v1 on v0

--- a/solution.py
+++ b/solution.py
@@ -37,7 +37,11 @@
         preferred_element_type=jnp.float32,
     )
     partial_value = partial_value.reshape(node_rows, feature_width)
-    result = lax.psum(partial_value, "rep")
+    n_dev = lax.axis_size("rep")
+    result, hop = (partial_value, 1)
+    while hop < n_dev:
+        result = result + lax.ppermute(result, "rep", [(i, i ^ hop) for i in range(n_dev)])
+        hop = 2 * hop
     return result
 
 

time: 662 us -> 633 us (0.956)
  blocking collectives: 26.8 us -> 0 us
    psum x2 -> x0, blocking collectives: 26.8 us -> none  [aggregate(): result = lax.psum(partial_value, 'rep')]
    ppermute x0 -> x6, waiting for transfers between devices: none -> 18.4 us  [aggregate(): lax.ppermute(result, 'rep', [(i, i ^ hop) for i in range(n_dev)])]
    psum x1 -> x0, waiting for transfers between devices: 17.9 us -> none  [aggregate(): result = lax.psum(partial_value, 'rep')]
  transfers between devices with their start and end apart: 8 -> 13, of which waited for: 8 -> 11; matrix products, arithmetic and copies ran while one was open for 1% -> 1% of each run, Pallas kernels for 0% -> 0%
where the time goes in v1:
time: 633 us
  waiting for transfers between devices  581 us (92%)
  local copies, waits for them, and re-layouts  16.4 us (3%)
  between operations  15.7 us (2%)
    psum x6, waiting for transfers between devices, broadcast(): return lax.psum(jnp.where(mine, array, jnp.zeros_like(array)), axis)  436 us
    psum x1, waiting for transfers between devices, shards(): grad_one = lax.psum(grad_one, ('row', 'rep'))  126 us
    ppermute x6, waiting for transfers between devices, aggregate(): lax.ppermute(result, 'rep', [(i, i ^ hop) for i in range(n_dev)])  18.4 us
  transfers between devices with their start and end apart: 13, of which 11 were waited for; matrix products, arithmetic and copies ran while one was open for 1% of the time, Pallas kernels for 0%

profile of v1, /device:TPU:0, one launch (start us, length us, event | category | flops | bytes accessed | tf_op | source)
XLA Modules:
  0.0 632.6 jit_solution(7113601868899990367)
XLA Ops:
  8.0 0.7 copy-done.4
  8.9 1.2 convolution_convert_fusion
  10.1 154.0 %while.38 = (s32[]{:T(128)}, bf16[2,256,256]{2,1,0:T(8,128)(2,1)S(1)}, s32[2]{0:T(128)S(1)}, s32[]{:T(128)}, bf16[256,256]{1,0:T(8,128)(2,1)S(1)}, /*index=5*/s32[]{:T(128)}, u32[]{:T(128)}, u32[]{:T(128)}) while((s32[]{:T(128)}, bf16[2,256,256]{2,1,0:T(8,128)(2,1)S(1)}, s32[2]{0:T(128)S(1)}, s32[]{:T(128)}, bf16[256,256]{1,0:T(8,128)(2,1)S(1)}, ...), condition=%wide.region_8.10_spmd, body=%wide.region_6.9_spmd.sunk | while | flops 131079 | bytes 1310923 | solution.py:25
  10.2 0.6 dynamic_slice.63
  11.4 0.7 select_bitcast_fusion.8
  12.1 75.9 %all-reduce.12.cloned.1.call-done = bf16[1,256,256]{2,1,0:T(8,128)(2,1)} async-done(((bf16[1,256,256]{2,1,0:T(8,128)(2,1)}), bf16[1,256,256]{2,1,0:T(8,128)(2,1)}) %all-reduce.12.cloned.1.call-update) | async-done | bytes 131088 | tf_op jit(solution)/shard_map/while/body/eval_jaxpr/psum | solution.py:9
  88.0 0.9 constant_dynamic-update-slice_fusion.8
  89.0 0.6 dynamic_slice.63
  90.2 0.7 select_bitcast_fusion.8
  90.9 72.3 %all-reduce.12.cloned.1.call-done = bf16[1,256,256]{2,1,0:T(8,128)(2,1)} async-done(((bf16[1,256,256]{2,1,0:T(8,128)(2,1)}), bf16[1,256,256]{2,1,0:T(8,128)(2,1)}) %all-reduce.12.cloned.1.call-update) | async-done | bytes 131088 | tf_op jit(solution)/shard_map/while/body/eval_jaxpr/psum | solution.py:9
  163.2 0.9 constant_dynamic-update-slice_fusion.8
  164.1 0.6 gather_fusion.2
  164.7 0.9 copy-done.1
  165.6 150.0 %while.36 = (s32[]{:T(128)}, bf16[2,256,256]{2,1,0:T(8,128)(2,1)S(1)}, s32[2]{0:T(128)S(1)}, s32[]{:T(128)}, bf16[256,256]{1,0:T(8,128)(2,1)S(1)}, /*index=5*/s32[]{:T(128)}, u32[]{:T(128)}, u32[]{:T(128)}) while((s32[]{:T(128)}, bf16[2,256,256]{2,1,0:T(8,128)(2,1)S(1)}, s32[2]{0:T(128)S(1)}, s32[]{:T(128)}, bf16[256,256]{1,0:T(8,128)(2,1)S(1)}, ...), condition=%wide.region_2.3_spmd, body=%wide.region_0.2_spmd.sunk | while | flops 131079 | bytes 1310923 | solution.py:25
  165.6 0.6 dynamic_slice.61
  166.8 0.7 select_bitcast_fusion.6
  167.5 72.3 %all-reduce.8.cloned.1.call-done = bf16[1,256,256]{2,1,0:T(8,128)(2,1)} async-done(((bf16[1,256,256]{2,1,0:T(8,128)(2,1)}), bf16[1,256,256]{2,1,0:T(8,128)(2,1)}) %all-reduce.8.cloned.1.call-update) | async-done | bytes 131088 | tf_op jit(solution)/shard_map/while/body/eval_jaxpr/psum | solution.py:9
  239.8 0.9 constant_dynamic-update-slice_fusion.6
  240.8 0.6 dynamic_slice.61
  242.1 0.7 select_bitcast_fusion.6
  242.8 71.9 %all-reduce.8.cloned.1.call-done = bf16[1,256,256]{2,1,0:T(8,128)(2,1)} async-done(((bf16[1,256,256]{2,1,0:T(8,128)(2,1)}), bf16[1,256,256]{2,1,0:T(8,128)(2,1)}) %all-reduce.8.cloned.1.call-update) | async-done | bytes 131088 | tf_op jit(solution)/shard_map/while/body/eval_jaxpr/psum | solution.py:9
  314.7 0.9 constant_dynamic-update-slice_fusion.6
  315.6 0.6 gather_fusion
  316.2 0.6 copy-done.6
  317.5 1.5 collective-permute-done
  319.1 1.5 collective-permute-start.1
  321.0 6.5 %collective-permute-done.1 = f32[256,256]{1,0:T(8,128)S(1)} collective-permute-done((f32[256,256]{1,0:T(8,128)S(1)}, f32[256,256]{1,0:T(8,128)S(1)}, u32[]{:S(2)}, u32[]{:S(2)}) %collective-permute-start.1) | collective-permute-done | bytes 262176 | tf_op jit(solution)/shard_map/ppermute | solution.py:43
  327.8 149.8 %while.37 = (s32[]{:T(128)}, bf16[2,256,256]{2,1,0:T(8,128)(2,1)S(1)}, s32[2]{0:T(128)S(1)}, s32[]{:T(128)}, bf16[256,256]{1,0:T(8,128)(2,1)S(1)}, /*index=5*/s32[]{:T(128)}, u32[]{:T(128)}, u32[]{:T(128)}) while((s32[]{:T(128)}, bf16[2,256,256]{2,1,0:T(8,128)(2,1)S(1)}, s32[2]{0:T(128)S(1)}, s32[]{:T(128)}, bf16[256,256]{1,0:T(8,128)(2,1)S(1)}, ...), condition=%wide.region_5.7_spmd, body=%wide.region_3.6_spmd.sunk | while | flops 131079 | bytes 1310923 | solution.py:25
  327.9 0.6 dynamic_slice.62
  329.1 0.7 select_bitcast_fusion.7
  329.8 72.0 %all-reduce.10.cloned.1.call-done = bf16[1,256,256]{2,1,0:T(8,128)(2,1)} async-done(((bf16[1,256,256]{2,1,0:T(8,128)(2,1)}), bf16[1,256,256]{2,1,0:T(8,128)(2,1)}) %all-reduce.10.cloned.1.call-update) | async-done | bytes 131088 | tf_op jit(solution)/shard_map/while/body/eval_jaxpr/psum | solution.py:9
  401.8 0.9 constant_dynamic-update-slice_fusion.7
  402.8 0.6 dynamic_slice.62
  404.0 0.7 select_bitcast_fusion.7
  404.7 71.9 %all-reduce.10.cloned.1.call-done = bf16[1,256,256]{2,1,0:T(8,128)(2,1)} async-done(((bf16[1,256,256]{2,1,0:T(8,128)(2,1)}), bf16[1,256,256]{2,1,0:T(8,128)(2,1)}) %all-reduce.10.cloned.1.call-update) | async-done | bytes 131088 | tf_op jit(solution)/shard_map/while/body/eval_jaxpr/psum | solution.py:9
  476.7 0.9 constant_dynamic-update-slice_fusion.7
  477.6 0.6 gather_fusion.1
  478.8 1.5 collective-permute-start.5
  480.4 1.5 collective-permute-start.3
  481.8 6.2 collective-permute-done.5
  488.0 0.9 fusion.18
  489.0 4.2 collective-permute-done.3
  493.2 1.7 fusion.20
  494.9 0.9 copy-done.2
  495.8 0.8 convolution_convert_fusion.1
  496.5 126.2 %all-reduce.6.cloned.1.call-done = (f32[256,256]{1,0:T(8,128)}, f32[256,256]{1,0:T(8,128)}) async-done(((f32[256,256]{1,0:T(8,128)}, f32[256,256]{1,0:T(8,128)}), (f32[256,256]{1,0:T(8,128)}, f32[256,256]{1,0:T(8,128)})) %all-reduce.6.cloned.1.call-update) | async-done | bytes 524304 | tf_op jit(solution)/shard_map/psum | solution.py:85
  622.8 1.7 copy.39
  624.5 0.7 copy.40
  (52 shorter events, 2.4 us)
Async XLA Ops:
  8.0 309.1 %copy-start = (bf16[1,1,2,4,128,128]{5,4,3,2,1,0:T(8,128)(2,1)S(1)}, bf16[1,1,2,4,128,128]{5,4,3,2,1,0:T(8,128)(2,1)}, u32[]{:S(2)}) copy-start(bf16[1,1,2,4,128,128]{5,4,3,2,1,0:T(8,128)(2,1)} %param.21) | copy-start | bytes 786436
  8.0 0.7 copy-start.4
  10.1 77.9 %all-reduce.12.cloned.1.call-start = ((), (), s32[]{:S(2)}) async-start(), calls=%async_computation.3 | async-start | bytes 262144 | tf_op jit(solution)/shard_map/while/body/eval_jaxpr/psum | solution.py:9
  88.9 74.3 %all-reduce.12.cloned.1.call-start = ((), (), s32[]{:S(2)}) async-start(), calls=%async_computation.3 | async-start | bytes 262144 | tf_op jit(solution)/shard_map/while/body/eval_jaxpr/psum | solution.py:9
  164.7 0.9 copy-start.1
  165.6 74.2 %all-reduce.8.cloned.1.call-start = ((), (), s32[]{:S(2)}) async-start(), calls=%async_computation.1 | async-start | bytes 262144 | tf_op jit(solution)/shard_map/while/body/eval_jaxpr/psum | solution.py:9
  240.8 73.9 %all-reduce.8.cloned.1.call-start = ((), (), s32[]{:S(2)}) async-start(), calls=%async_computation.1 | async-start | bytes 262144 | tf_op jit(solution)/shard_map/while/body/eval_jaxpr/psum | solution.py:9
  316.2 0.7 copy-start.6
  317.4 1.6 collective-permute-start
  319.1 8.4 %collective-permute-start.1 = (f32[256,256]{1,0:T(8,128)S(1)}, f32[256,256]{1,0:T(8,128)S(1)}, u32[]{:S(2)}, u32[]{:S(2)}) collective-permute-start(f32[256,256]{1,0:T(8,128)S(1)} %bitcast_add_fusion.2), channel_id=1, source_target_pairs={{0,2},{1,3},{2,0},{3,1},{4,6},{5,7},{6,4},{7,5},{8,10},{9,11},{10,... | collective-permute-start | bytes 786440 | tf_op jit(solution)/shard_map/ppermute | solution.py:43
  320.9 157.8 %collective-permute-start.4 = (f32[256,256]{1,0:T(8,128)S(1)}, f32[256,256]{1,0:T(8,128)S(1)}, u32[]{:S(2)}, u32[]{:S(2)}) collective-permute-start(f32[256,256]{1,0:T(8,128)S(1)} %bitcast.69), channel_id=1, source_target_pairs={{0,1},{1,0},{2,3},{3,2},{4,5},{5,4},{6,7},{7,6},{8,9},{9,8},{10,11... | collective-permute-start | bytes 786440 | tf_op jit(solution)/shard_map/ppermute | solution.py:43
  321.0 6.5 %copy-start.5 = (bf16[256,256]{1,0:T(8,128)(2,1)S(1)}, bf16[256,256]{1,0:T(8,128)(2,1)}, u32[]{:S(2)}) copy-start(bf16[256,256]{1,0:T(8,128)(2,1)} %param.17) | copy-start | bytes 393220
  327.8 74.0 %all-reduce.10.cloned.1.call-start = ((), (), s32[]{:S(2)}) async-start(), calls=%async_computation.2 | async-start | bytes 262144 | tf_op jit(solution)/shard_map/while/body/eval_jaxpr/psum | solution.py:9
  402.7 73.9 %all-reduce.10.cloned.1.call-start = ((), (), s32[]{:S(2)}) async-start(), calls=%async_computation.2 | async-start | bytes 262144 | tf_op jit(solution)/shard_map/while/body/eval_jaxpr/psum | solution.py:9
  477.6 145.2 %all-reduce.6.cloned.1.call-start = ((), (), s32[]{:S(2)}) async-start(), calls=%async_computation | async-start | bytes 1048576 | tf_op jit(solution)/shard_map/psum | solution.py:85
  478.7 1.7 collective-permute-start.2
  478.8 9.2 %collective-permute-start.5 = (f32[256,256]{1,0:T(8,128)S(1)}, f32[256,256]{1,0:T(8,128)S(1)}, u32[]{:S(2)}, u32[]{:S(2)}) collective-permute-start(f32[256,256]{1,0:T(8,128)S(1)} %bitcast_add_fusion), channel_id=1, source_target_pairs={{0,2},{1,3},{2,0},{3,1},{4,6},{5,7},{6,4},{7,5},{8,10},{9,11},{10,... | collective-permute-start | bytes 786440 | tf_op jit(solution)/shard_map/ppermute | solution.py:43
  480.4 12.8 %collective-permute-start.3 = (f32[256,256]{1,0:T(8,128)S(1)}, f32[256,256]{1,0:T(8,128)S(1)}, u32[]{:S(2)}, u32[]{:S(2)}) collective-permute-start(f32[256,256]{1,0:T(8,128)S(1)} %bitcast_add_fusion.1), channel_id=1, source_target_pairs={{0,2},{1,3},{2,0},{3,1},{4,6},{5,7},{6,4},{7,5},{8,10},{9,11},{10,... | collective-permute-start | bytes 786440 | tf_op jit(solution)/shard_map/ppermute | solution.py:43
  494.9 0.9 copy-start.2
  622.8 1.7 copy-start.3
Sparse Core Ops, SparseCore 0:
  14.8 73.1 all-reduce.11
  93.6 69.4 all-reduce.11
  170.3 69.4 all-reduce.7
  245.2 69.4 all-reduce.7
  332.2 69.5 all-reduce.9
  407.1 69.4 all-reduce.9
Sparse Core Ops, SparseCore 1:
  495.0 127.7 all-reduce.5
